TPU v7x, 256 devices: a whole 4x4x8 slice. The times are simulated.
256 devices in a mesh: prompt: 16 (over x_hi, z), resp: 8 (over x_lo, y), head: 2 (over core).
Axes of the slice: x: 4 (x_hi: 2, x_lo: 2; x = x_hi * 2 + x_lo), y: 4, z: 8, core: 2. Of those that a mesh axis runs over, the one named last changes fastest.
Arguments:
- prompt_q: bfloat16 [8, 1024, 4, 512], P('resp', 'prompt', None, 'head'), may hold values from -250 to 250
- prompt_kv: bfloat16 [2, 8, 1024, 512], P(None, 'resp', 'prompt'), may hold values from -8 to 8
- prompt_grad: bfloat16 [8, 1024, 4, 512], P('resp', 'prompt', None, 'head'), may hold values from -6 to 6
- resp_q: bfloat16 [16, 8, 8, 64, 4, 512], P('prompt', 'resp', None, None, None, 'head'), may hold values from -250 to 250
- resp_kv: bfloat16 [2, 16, 8, 8, 64, 512], P(None, 'prompt', 'resp'), may hold values from -6 to 6
- resp_grad: bfloat16 [16, 8, 8, 64, 4, 512], P('prompt', 'resp', None, None, None, 'head'), may hold values from -6 to 6
- resp_prompt: int32 [16, 8, 8], P('prompt', 'resp'), may hold values from 0 to 7, as said below
Outputs:
- prompt_out: bfloat16 [8, 1024, 4, 512], P('resp', 'prompt', None, 'head')
- prompt_dq: bfloat16 [8, 1024, 4, 512], P('resp', 'prompt', None, 'head')
- prompt_dkv: bfloat16 [2, 8, 1024, 512], P(None, 'resp', 'prompt', 'head')
- resp_out: bfloat16 [16, 8, 8, 64, 4, 512], P('prompt', 'resp', None, None, None, 'head')
- resp_dq: bfloat16 [16, 8, 8, 64, 4, 512], P('prompt', 'resp', None, None, None, 'head')
- resp_dkv: bfloat16 [2, 16, 8, 8, 64, 512], P(None, 'prompt', 'resp', None, None, 'head')
Inputs may be any that keep to these rules, and one draw needn't show every extreme that they name: `resp_prompt`: entry [p, r, j] is the prompt of response j held at prompt index p and resp index r; each row of 8 entries names every prompt once.
All inputs are finite; a program needn't handle non-finite values.
Results may differ from a plain program's by a relative error of at most 0.0095.
Values may be sent and summed in bfloat16 or wider, within the bound.
No kernel may reach another device: no remote copies, remote signals or barrier semaphores. Data moves between devices by JAX's collectives and lax.ppermute only.
A program may use at most 128 MiB of HBM per device.

v0:
```python
import math
import jax
import jax.numpy as jnp
from jax import lax
from jax.sharding import PartitionSpec as P

HD = 128


def attend_blocks(queries, keys_in, values_in, own_keys, own_values, cotangent, shared_ok, own_ok):
    scale = 1.0 / math.sqrt(HD)
    f32 = jnp.float32
    s_sh = jnp.einsum("brkgd,nkd->bkgrn", queries, keys_in, preferred_element_type=f32) * scale
    s_own = jnp.einsum("brkgd,bukd->bkgru", queries, own_keys, preferred_element_type=f32) * scale
    s_sh = jnp.where(shared_ok[:, None, None], s_sh, -1e30)
    s_own = jnp.where(own_ok[:, None, None], s_own, -1e30)
    row_max = jnp.maximum(
        jnp.max(s_sh, axis=-1, keepdims=True), jnp.max(s_own, axis=-1, keepdims=True)
    )
    totals = jnp.sum(jnp.exp(s_sh - row_max), axis=-1, keepdims=True) + jnp.sum(
        jnp.exp(s_own - row_max), axis=-1, keepdims=True
    )
    log_total = row_max + jnp.log(totals)
    p_sh = jnp.exp(s_sh - log_total)
    p_own = jnp.exp(s_own - log_total)
    w_sh = p_sh.astype(jnp.bfloat16)
    w_own = p_own.astype(jnp.bfloat16)
    output = (
        jnp.einsum("bkgrn,nkd->brkgd", w_sh, values_in, preferred_element_type=f32)
        + jnp.einsum("bkgru,bukd->brkgd", w_own, own_values, preferred_element_type=f32)
    ).astype(jnp.bfloat16)
    row_delta = jnp.einsum("brkgd,brkgd->bkgr", cotangent, output, preferred_element_type=f32)
    dp_sh = jnp.einsum("brkgd,nkd->bkgrn", cotangent, values_in, preferred_element_type=f32)
    dp_own = jnp.einsum("brkgd,bukd->bkgru", cotangent, own_values, preferred_element_type=f32)
    ds_sh = (p_sh * (dp_sh - row_delta[..., None])).astype(jnp.bfloat16)
    ds_own = (p_own * (dp_own - row_delta[..., None])).astype(jnp.bfloat16)
    dquery = (
        jnp.einsum("bkgrn,nkd->brkgd", ds_sh, keys_in, preferred_element_type=f32)
        + jnp.einsum("bkgru,bukd->brkgd", ds_own, own_keys, preferred_element_type=f32)
    ) * scale
    dk_sh = jnp.einsum("bkgrn,brkgd->nkd", ds_sh, queries, preferred_element_type=f32) * scale
    dv_sh = jnp.einsum("bkgrn,brkgd->nkd", w_sh, cotangent, preferred_element_type=f32)
    dk_own = jnp.einsum("bkgru,brkgd->bukd", ds_own, queries, preferred_element_type=f32) * scale
    dv_own = jnp.einsum("bkgru,brkgd->bukd", w_own, cotangent, preferred_element_type=f32)
    return (output, dquery, dk_sh, dv_sh, dk_own, dv_own)


def body(prompt_q, prompt_kv, prompt_grad, resp_q, resp_kv, resp_grad, resp_prompt):
    head_size = HD
    block_rows = prompt_q.shape[1]
    kv_heads = prompt_q.shape[2]
    local_width = prompt_q.shape[3]
    local_heads = local_width // head_size
    full_len = block_rows * lax.axis_size("prompt")
    resp_len = resp_q.shape[3]
    peers = lax.axis_size("resp")
    kv_width = kv_heads * head_size
    gathered = lax.all_gather(prompt_kv, "prompt", axis=2, tiled=True)
    prompt_keys = gathered[0, 0].reshape(full_len, kv_heads, head_size)
    prompt_values = gathered[1, 0].reshape(full_len, kv_heads, head_size)
    order = resp_prompt[0, 0]
    picker = (jnp.arange(peers)[:, None] == order[None, :]).astype(jnp.bfloat16)
    send_q = jnp.einsum(
        "dj,jrkh->drkh", picker, resp_q[0, 0], preferred_element_type=jnp.float32
    ).astype(jnp.bfloat16)
    send_kv = jnp.einsum(
        "dj,cjrh->dcrh", picker, resp_kv[:, 0, 0], preferred_element_type=jnp.float32
    ).astype(jnp.bfloat16)
    send_grad = jnp.einsum(
        "dj,jrkh->drkh", picker, resp_grad[0, 0], preferred_element_type=jnp.float32
    ).astype(jnp.bfloat16)
    got_q, got_kv, got_grad = (
        lax.all_to_all(send_q, "resp", split_axis=0, concat_axis=0, tiled=True),
        lax.all_to_all(send_kv, "resp", split_axis=0, concat_axis=0, tiled=True),
        lax.all_to_all(send_grad, "resp", split_axis=0, concat_axis=0, tiled=True),
    )
    q_shape = (peers + 1, resp_len, kv_heads, local_heads, head_size)
    queries = jnp.concatenate([got_q, prompt_q], axis=0).reshape(q_shape)
    cotangent = jnp.concatenate([got_grad, prompt_grad], axis=0).reshape(q_shape)
    own_kv = jnp.concatenate(
        [got_kv, jnp.zeros((1,) + got_kv.shape[1:], got_kv.dtype)], axis=0
    ).reshape(peers + 1, 2, resp_len, kv_heads, head_size)
    query_rows = lax.axis_index("prompt") * block_rows + jnp.arange(block_rows)
    key_cols = jnp.arange(full_len)
    causal = key_cols[None, :] <= query_rows[:, None]
    shared_ok = jnp.concatenate([jnp.ones((peers, resp_len, full_len), bool), causal[None]], axis=0)
    steps_own = jnp.arange(resp_len)
    own_causal = steps_own[None, :] <= steps_own[:, None]
    own_ok = jnp.concatenate(
        [
            jnp.broadcast_to(own_causal, (peers, resp_len, resp_len)),
            jnp.zeros((1, resp_len, resp_len), bool),
        ],
        axis=0,
    )
    out, dq, dk_sh, dv_sh, dk_own, dv_own = attend_blocks(
        queries,
        prompt_keys,
        prompt_values,
        own_kv[:, 0],
        own_kv[:, 1],
        cotangent,
        shared_ok,
        own_ok,
    )
    out = out.reshape(peers + 1, resp_len, kv_heads, local_width)
    dq = dq.astype(jnp.bfloat16).reshape(peers + 1, resp_len, kv_heads, local_width)
    prompt_part = jnp.stack([dk_sh, dv_sh]).reshape(2, full_len, kv_width)
    head_sum = lax.psum_scatter(prompt_part, "head", scatter_dimension=2, tiled=True)
    block_sum = lax.psum_scatter(head_sum, "prompt", scatter_dimension=1, tiled=True)
    own_part = jnp.stack([dk_own[:peers], dv_own[:peers]], axis=1).reshape(
        peers, 2, resp_len, kv_width
    )
    own_sum = lax.psum_scatter(own_part, "head", scatter_dimension=3, tiled=True)
    prompt_dkv = block_sum.astype(jnp.bfloat16)[:, None]
    back_kv = own_sum.astype(jnp.bfloat16)
    ret_out, ret_dq, ret_kv = (
        lax.all_to_all(out[:peers], "resp", split_axis=0, concat_axis=0, tiled=True),
        lax.all_to_all(dq[:peers], "resp", split_axis=0, concat_axis=0, tiled=True),
        lax.all_to_all(back_kv, "resp", split_axis=0, concat_axis=0, tiled=True),
    )
    resp_out = jnp.einsum(
        "dj,drkh->jrkh", picker, ret_out, preferred_element_type=jnp.float32
    ).astype(jnp.bfloat16)[None, None]
    resp_dq = jnp.einsum(
        "dj,drkh->jrkh", picker, ret_dq, preferred_element_type=jnp.float32
    ).astype(jnp.bfloat16)[None, None]
    resp_dkv = jnp.einsum(
        "dj,dcrh->cjrh", picker, ret_kv, preferred_element_type=jnp.float32
    ).astype(jnp.bfloat16)[:, None, None]
    prompt_out = out[peers:]
    prompt_dq = dq[peers:]
    return (prompt_out, prompt_dq, prompt_dkv, resp_out, resp_dq, resp_dkv)


def solution(mesh):
    return jax.shard_map(
        body,
        mesh=mesh,
        in_specs=(
            P("resp", "prompt", None, "head"),
            P(None, "resp", "prompt", None),
            P("resp", "prompt", None, "head"),
            P("prompt", "resp", None, None, None, "head"),
            P(None, "prompt", "resp", None, None, None),
            P("prompt", "resp", None, None, None, "head"),
            P("prompt", "resp", None),
        ),
        out_specs=(
            P("resp", "prompt", None, "head"),
            P("resp", "prompt", None, "head"),
            P(None, "resp", "prompt", "head"),
            P("prompt", "resp", None, None, None, "head"),
            P("prompt", "resp", None, None, None, "head"),
            P(None, "prompt", "resp", None, None, "head"),
        ),
        check_vma=False,
    )
```

profile of v0, /device:TPU:8, one launch (start us, length us, event | category | flops | bytes accessed | tf_op | source)
XLA Modules:
  0.0 434.3 jit_solution(9284214201687019022)
XLA Ops:
  11.9 5.8 %all-to-all-start = ((bf16[8,64,4,256]{3,2,1,0:T(4,128)(2,1)}), bf16[8,64,4,256]{3,2,1,0:T(4,128)(2,1)S(1)}, u32[]{:S(2)}, u32[]{:S(2)}) async-start(bf16[8,64,4,256]{3,2,1,0:T(4,128)(2,1)} %copy.205), calls=%async_computation | async-start | bytes 2097152 | tf_op jit(solution)/shard_map/all_to_all | solution.py:73
  19.8 12.4 %all-to-all-done = bf16[8,64,4,256]{3,2,1,0:T(4,128)(2,1)S(1)} async-done(((bf16[8,64,4,256]{3,2,1,0:T(4,128)(2,1)}), bf16[8,64,4,256]{3,2,1,0:T(4,128)(2,1)S(1)}, u32[]{:S(2)}, u32[]{:S(2)}) %all-to-all-start) | async-done | bytes 1048608 | tf_op jit(solution)/shard_map/all_to_all | solution.py:73
  32.2 4.8 %all-to-all-start.1 = ((bf16[8,2,64,512]{3,2,1,0:T(8,128)(2,1)}), bf16[8,2,64,512]{3,2,1,0:T(8,128)(2,1)S(1)}, u32[]{:S(2)}, u32[]{:S(2)}) async-start(bf16[8,2,64,512]{3,2,1,0:T(8,128)(2,1)} %copy.213), calls=%async_computation.1 | async-start | bytes 2097152 | tf_op jit(solution)/shard_map/all_to_all | solution.py:74
  39.2 10.8 %all-to-all-done.1 = bf16[8,2,64,512]{3,2,1,0:T(8,128)(2,1)S(1)} async-done(((bf16[8,2,64,512]{3,2,1,0:T(8,128)(2,1)}), bf16[8,2,64,512]{3,2,1,0:T(8,128)(2,1)S(1)}, u32[]{:S(2)}, u32[]{:S(2)}) %all-to-all-start.1) | async-done | bytes 1048608 | tf_op jit(solution)/shard_map/all_to_all | solution.py:74
  50.0 5.3 %all-to-all-start.2 = ((bf16[8,64,4,256]{3,2,1,0:T(4,128)(2,1)}), bf16[8,64,4,256]{3,2,1,0:T(4,128)(2,1)}, u32[]{:S(2)}, u32[]{:S(2)}) async-start(bf16[8,64,4,256]{3,2,1,0:T(4,128)(2,1)} %copy.231), calls=%async_computation.2 | async-start | bytes 2097152 | tf_op jit(solution)/shard_map/all_to_all | solution.py:75
  60.2 12.0 %all-to-all-done.2 = bf16[8,64,4,256]{3,2,1,0:T(4,128)(2,1)} async-done(((bf16[8,64,4,256]{3,2,1,0:T(4,128)(2,1)}), bf16[8,64,4,256]{3,2,1,0:T(4,128)(2,1)}, u32[]{:S(2)}, u32[]{:S(2)}) %all-to-all-start.2) | async-done | bytes 1048608 | tf_op jit(solution)/shard_map/all_to_all | solution.py:75
  82.6 21.9 %all-gather.2.cloned.1.call-done = bf16[2,1,1024,512]{3,0,1,2:T(2,128)(2,1)} async-done(((bf16[2,1,64,512]{3,0,1,2:T(2,128)(2,1)}), bf16[2,1,1024,512]{3,0,1,2:T(2,128)(2,1)}) %all-gather.2.cloned.1.call-update) | async-done | bytes 2097168 | tf_op jit(solution)/shard_map/all_gather | solution.py:58
  104.5 6.9 %fusion.60 = (bf16[1,1,1024,512]{3,0,1,2:T(2,128)(2,1)}, bf16[1,1,1024,512]{3,0,1,2:T(2,128)(2,1)}) fusion(bf16[2,1,1024,512]{3,0,1,2:T(2,128)(2,1)} %all-gather.2.cloned.1.call-done), kind=kLoop, calls=%fused_computation.87 | loop fusion | bytes 4194304 | tf_op jit(solution)/shard_map/slice | solution.py:60
  111.4 5.8 %copy.323 = bf16[1,1,1024,512]{2,3,1,0:T(8,128)(2,1)} copy(bf16[1,1,1024,512]{3,0,1,2:T(2,128)(2,1)} %get-tuple-element.37) | data formatting | bytes 2097152
  117.2 5.6 %bitcast_reduce_fusion = (f32[9,4,2,64]{3,2,0,1:T(2,128)S(1)}, f32[4,9,64,2,1024]{4,2,3,1,0:T(8,128)S(1)}) fusion(pred[9,64,1024]{2,1,0:T(8,128)(4,1)} %concatenate.17, bf16[1024,4,128,1,1]{0,2,4,3,1:T(8,128)(2,1)} %bitcast.155, bf16[9,64,4,2,128]{4,3,2,1,0:T(2,128)(2,1)} %reshape.116), kind=kOutput, calls=%fused_computation.5 | convolution fusion | flops 1222110720 | bytes 21710848 | tf_op jit(solution)/shard_map/brkgd,nkd->bkgrn/dot_general | solution.py:13
  122.9 5.4 %fusion.3 = f32[9,4,2,64]{3,2,0,1:T(2,128)S(1)} fusion(f32[4,9,64,2,1024]{4,2,3,1,0:T(8,128)S(1)} %get-tuple-element.43, f32[9,4,2,64]{3,2,0,1:T(2,128)S(1)} %copy.218, pred[9,64,1024]{2,1,0:T(8,128)(4,1)S(1)} %copy-done.13), kind=kLoop, calls=%fused_computation.7 | loop fusion | flops 18869760 | bytes 19501056 | tf_op jit(solution)/shard_map/reduce_sum | solution.py:20
  130.0 5.8 %copy.325 = bf16[1,1,1024,512]{2,3,1,0:T(8,128)(2,1)} copy(bf16[1,1,1024,512]{3,0,1,2:T(2,128)(2,1)} %get-tuple-element.36) | data formatting | bytes 2097152
  135.8 10.9 %fusion.28 = f32[4,128,1024,1,1]{2,1,4,3,0:T(8,128)} fusion(bf16[9,64,4,2,128]{4,3,2,1,0:T(2,128)(2,1)} %copy-done.6, f32[4,9,64,2,1024]{4,2,3,1,0:T(8,128)} %copy-done.5, f32[9,4,2,64]{3,2,0,1:T(2,128)S(1)} %copy.222, pred[9,64,1024]{2,1,0:T(8,128)(4,1)} %concatenate.17), kind=kOutput, calls=%fused_computation.54 | convolution fusion | flops 1226833920 | bytes 22759424 | tf_op jit(solution)/shard_map/bkgrn,brkgd->nkd/dot_general | solution.py:42
  148.8 10.0 %multiply_reduce_fusion = (f32[9,4,2,64]{3,2,0,1:T(2,128)S(1)}, bf16[9,64,4,2,128]{4,1,3,0,2:T(8,128)(2,1)}) fusion(f32[9,4,2,64,128]{4,2,3,1,0:T(2,128)S(1)} %copy-done.16, f32[9,4,128,2,64]{2,4,3,0,1:T(8,128)S(1)} %fusion.19, bf16[1024,4,128,1,1]{0,2,4,3,1:T(8,128)(2,1)S(1)} %bitcast.159, f32[4,9,64,2,1024]{4,2,3,1,0:T(8,128)} %copy-done.5, ...), kind=kOutput, calls=%fused_computation.21 | convolution fusion | flops 1229778432 | bytes 26447872 | tf_op jit(solution)/shard_map/bkgrn,nkd->brkgd/dot_general | solution.py:29
  158.9 10.1 %fusion.1 = bf16[9,4,2,64,1024]{4,3,2,0,1:T(8,128)(2,1)S(1)} fusion(f32[4,9,64,2,1024]{4,2,3,1,0:T(8,128)} %copy-done.5, f32[9,4,2,64]{3,2,0,1:T(2,128)S(1)} %get-tuple-element.44, f32[9,4,2,64]{3,2,0,1:T(2,128)S(1)} %copy.222, pred[9,64,1024]{2,1,0:T(8,128)(4,1)S(1)} %copy-done.15, bf16[1024,4,128,1,1]{0,2,4,3,1:T(8,128)(2,1)} %bitcast.158, ...), kind=kOutput, calls=%fused_computation.2 | convolution fusion | flops 1236271104 | bytes 31166464 | tf_op jit(solution)/shard_map/brkgd,nkd->bkgrn/dot_general | solution.py:33
  169.0 5.2 %bitcast_multiply_fusion = f32[4,128,1024]{2,1,0:T(8,128)} fusion(bf16[9,4,2,64,1024]{4,3,2,0,1:T(8,128)(2,1)S(1)} %fusion.1, bf16[9,64,4,2,128]{4,3,2,1,0:T(2,128)(2,1)} %reshape.116), kind=kOutput, calls=%fused_computation.25 | convolution fusion | flops 1208483840 | bytes 12713984 | tf_op jit(solution)/shard_map/bkgrn,brkgd->nkd/dot_general | solution.py:41
  179.0 4.1 pad_maximum_fusion
  200.2 6.3 %fusion.7 = bf16[9,64,4,2,128]{4,1,3,0,2:T(8,128)(2,1)S(1)} fusion(f32[9,4,128,2,64]{2,4,3,0,1:T(8,128)S(1)} %fusion.17, bf16[9,4,2,64,1024]{4,3,2,0,1:T(8,128)(2,1)} %copy-done.2, bf16[1024,4,128,1,1]{0,2,4,3,1:T(8,128)(2,1)S(1)} %bitcast.156), kind=kOutput, calls=%fused_computation.14 | convolution fusion | flops 1209729024 | bytes 14024704 | tf_op jit(solution)/shard_map/bkgrn,nkd->brkgd/dot_general | solution.py:38
  209.2 5.5 %all-to-all-start.4 = ((bf16[8,64,4,256]{3,2,1,0:T(4,128)(2,1)}), bf16[8,64,4,256]{3,2,1,0:T(4,128)(2,1)S(1)}, u32[]{:S(2)}, u32[]{:S(2)}) async-start(bf16[8,64,4,256]{3,2,1,0:T(4,128)(2,1)} %reshape.121), calls=%async_computation.6 | async-start | bytes 2097152 | tf_op jit(solution)/shard_map/all_to_all | solution.py:119
  217.3 9.8 %all-to-all-done.4 = bf16[8,64,4,256]{3,2,1,0:T(4,128)(2,1)S(1)} async-done(((bf16[8,64,4,256]{3,2,1,0:T(4,128)(2,1)}), bf16[8,64,4,256]{3,2,1,0:T(4,128)(2,1)S(1)}, u32[]{:S(2)}, u32[]{:S(2)}) %all-to-all-start.4) | async-done | bytes 1048608 | tf_op jit(solution)/shard_map/all_to_all | solution.py:119
  227.1 4.8 %all-to-all-start.3 = ((bf16[8,64,4,256]{3,2,1,0:T(4,128)(2,1)}), bf16[8,64,4,256]{3,2,1,0:T(4,128)(2,1)S(1)}, u32[]{:S(2)}, u32[]{:S(2)}) async-start(bf16[8,64,4,256]{3,2,1,0:T(4,128)(2,1)} %reshape.120), calls=%async_computation.5 | async-start | bytes 2097152 | tf_op jit(solution)/shard_map/all_to_all | solution.py:118
  234.1 12.6 %all-to-all-done.3 = bf16[8,64,4,256]{3,2,1,0:T(4,128)(2,1)S(1)} async-done(((bf16[8,64,4,256]{3,2,1,0:T(4,128)(2,1)}), bf16[8,64,4,256]{3,2,1,0:T(4,128)(2,1)S(1)}, u32[]{:S(2)}, u32[]{:S(2)}) %all-to-all-start.3) | async-done | bytes 1048608 | tf_op jit(solution)/shard_map/all_to_all | solution.py:118
  246.7 5.2 %all-to-all-start.5 = ((bf16[8,2,64,256]{3,2,1,0:T(8,128)(2,1)}), bf16[8,2,64,256]{3,2,1,0:T(8,128)(2,1)}, u32[]{:S(2)}, u32[]{:S(2)}) async-start(bf16[8,2,64,256]{3,2,1,0:T(8,128)(2,1)} %copy.256), calls=%async_computation.8 | async-start | bytes 1048576 | tf_op jit(solution)/shard_map/all_to_all | solution.py:120
  261.7 164.3 %reduce-scatter.6.cloned.1.call-done = f32[2,64,256]{2,1,0:T(8,128)} async-done(((f32[2,1024,256]{2,1,0:T(8,128)}), f32[2,64,256]{2,1,0:T(8,128)}) %reduce-scatter.6.cloned.1.call-update) | async-done | bytes 131088 | tf_op jit(solution)/shard_map/reduce_scatter | solution.py:110
  (129 shorter events, 68.5 us)
Async XLA Ops:
  7.2 97.3 %all-gather.2.cloned.1.call-start = ((), (), s32[]{:S(2)}) async-start(), calls=%async_computation.9 | async-start | bytes 2228224 | tf_op jit(solution)/shard_map/all_gather | solution.py:58
  10.5 7.2 %copy-start.21 = (bf16[2,1,1,8,64,512]{5,4,3,2,1,0:T(8,128)(2,1)S(1)}, bf16[2,1,1,8,64,512]{5,4,3,2,1,0:T(8,128)(2,1)}, u32[]{:S(2)}) copy-start(bf16[2,1,1,8,64,512]{5,4,3,2,1,0:T(8,128)(2,1)} %param.11) | copy-start | bytes 3145732
  10.5 7.2 %copy-start.26 = (s32[1,1,8]{2,1,0:T(1,128)S(1)}, s32[1,1,8]{2,1,0:T(1,128)}, u32[]{:S(2)}) copy-start(s32[1,1,8]{2,1,0:T(1,128)} %param.13) | copy-start | bytes 100
  11.9 20.3 %all-to-all-start = ((bf16[8,64,4,256]{3,2,1,0:T(4,128)(2,1)}), bf16[8,64,4,256]{3,2,1,0:T(4,128)(2,1)S(1)}, u32[]{:S(2)}, u32[]{:S(2)}) async-start(bf16[8,64,4,256]{3,2,1,0:T(4,128)(2,1)} %copy.205), calls=%async_computation | async-start | bytes 2097152 | tf_op jit(solution)/shard_map/all_to_all | solution.py:73
  18.5 18.5 %copy-start.22 = (bf16[1,1,8,64,4,256]{5,4,3,2,1,0:T(4,128)(2,1)S(1)}, bf16[1,1,8,64,4,256]{5,4,3,2,1,0:T(4,128)(2,1)}, u32[]{:S(2)}) copy-start(bf16[1,1,8,64,4,256]{5,4,3,2,1,0:T(4,128)(2,1)} %param.12) | copy-start | bytes 3145732
  32.2 17.8 %all-to-all-start.1 = ((bf16[8,2,64,512]{3,2,1,0:T(8,128)(2,1)}), bf16[8,2,64,512]{3,2,1,0:T(8,128)(2,1)S(1)}, u32[]{:S(2)}, u32[]{:S(2)}) async-start(bf16[8,2,64,512]{3,2,1,0:T(8,128)(2,1)} %copy.213), calls=%async_computation.1 | async-start | bytes 2097152 | tf_op jit(solution)/shard_map/all_to_all | solution.py:74
  37.8 19.3 %copy-start.23 = (bf16[1,64,4,256]{3,2,1,0:T(4,128)(2,1)S(1)}, bf16[1,64,4,256]{3,2,1,0:T(4,128)(2,1)}, u32[]{:S(2)}) copy-start(bf16[1,64,4,256]{3,2,1,0:T(4,128)(2,1)} %param.7) | copy-start | bytes 393220
  50.0 22.2 %all-to-all-start.2 = ((bf16[8,64,4,256]{3,2,1,0:T(4,128)(2,1)}), bf16[8,64,4,256]{3,2,1,0:T(4,128)(2,1)}, u32[]{:S(2)}, u32[]{:S(2)}) async-start(bf16[8,64,4,256]{3,2,1,0:T(4,128)(2,1)} %copy.231), calls=%async_computation.2 | async-start | bytes 2097152 | tf_op jit(solution)/shard_map/all_to_all | solution.py:75
  55.3 142.4 %reduce-scatter.4.cloned.1.call-start = ((), (), s32[]{:S(2)}) async-start(), calls=%async_computation.10 | async-start | bytes 6291456 | tf_op jit(solution)/shard_map/reduce_scatter | solution.py:109
  59.7 12.5 %copy-start.24 = (bf16[1,64,4,256]{3,2,1,0:T(4,128)(2,1)S(1)}, bf16[1,64,4,256]{3,2,1,0:T(4,128)(2,1)}, u32[]{:S(2)}) copy-start(bf16[1,64,4,256]{3,2,1,0:T(4,128)(2,1)} %param.9) | copy-start | bytes 393220
  78.1 3.2 copy-start.6
  78.6 2.7 copy-start.17
  82.6 64.1 %copy-start.3 = (f32[9,4,2,64,64]{3,4,2,1,0:T(8,128)}, f32[9,4,2,64,64]{3,4,2,1,0:T(8,128)S(1)}, u32[]{:S(2)}) copy-start(f32[9,4,2,64,64]{3,4,2,1,0:T(8,128)S(1)} %get-tuple-element.41) | copy-start | bytes 3538948
  117.2 5.7 %copy-start.13 = (pred[9,64,1024]{2,1,0:T(8,128)(4,1)S(1)}, pred[9,64,1024]{2,1,0:T(8,128)(4,1)}, u32[]{:S(2)}) copy-start(pred[9,64,1024]{2,1,0:T(8,128)(4,1)} %concatenate.17) | copy-start | bytes 1769476
  122.8 6.4 %copy-start.5 = (f32[4,9,64,2,1024]{4,2,3,1,0:T(8,128)}, f32[4,9,64,2,1024]{4,2,3,1,0:T(8,128)S(1)}, u32[]{:S(2)}) copy-start(f32[4,9,64,2,1024]{4,2,3,1,0:T(8,128)S(1)} %get-tuple-element.43) | copy-start | bytes 56623108
  148.8 10.0 %copy-start.15 = (pred[9,64,1024]{2,1,0:T(8,128)(4,1)S(1)}, pred[9,64,1024]{2,1,0:T(8,128)(4,1)}, u32[]{:S(2)}) copy-start(pred[9,64,1024]{2,1,0:T(8,128)(4,1)} %concatenate.17) | copy-start | bytes 1769476
  169.0 5.2 %copy-start.2 = (bf16[9,4,2,64,1024]{4,3,2,0,1:T(8,128)(2,1)}, bf16[9,4,2,64,1024]{4,3,2,0,1:T(8,128)(2,1)S(1)}, u32[]{:S(2)}) copy-start(bf16[9,4,2,64,1024]{4,3,2,0,1:T(8,128)(2,1)S(1)} %fusion.1) | copy-start | bytes 28311556
  183.2 48.8 %reduce-scatter.8.cloned.1.call-start = ((), (), s32[]{:S(2)}) async-start(), calls=%async_computation.12 | async-start | bytes 3145728 | tf_op jit(solution)/shard_map/reduce_scatter | solution.py:114
  197.6 228.4 %reduce-scatter.6.cloned.1.call-start = ((), (), s32[]{:S(2)}) async-start(), calls=%async_computation.11 | async-start | bytes 2228224 | tf_op jit(solution)/shard_map/reduce_scatter | solution.py:110
  207.7 7.0 %copy-start.19 = (bf16[9,64,4,2,128]{4,1,3,0,2:T(8,128)(2,1)S(1)}, bf16[9,64,4,2,128]{4,1,3,0,2:T(8,128)(2,1)}, u32[]{:S(2)}) copy-start(bf16[9,64,4,2,128]{4,1,3,0,2:T(8,128)(2,1)} %get-tuple-element.45) | copy-start | bytes 3538948
  209.2 18.0 %all-to-all-start.4 = ((bf16[8,64,4,256]{3,2,1,0:T(4,128)(2,1)}), bf16[8,64,4,256]{3,2,1,0:T(4,128)(2,1)S(1)}, u32[]{:S(2)}, u32[]{:S(2)}) async-start(bf16[8,64,4,256]{3,2,1,0:T(4,128)(2,1)} %reshape.121), calls=%async_computation.6 | async-start | bytes 2097152 | tf_op jit(solution)/shard_map/all_to_all | solution.py:119
  227.1 19.5 %all-to-all-start.3 = ((bf16[8,64,4,256]{3,2,1,0:T(4,128)(2,1)}), bf16[8,64,4,256]{3,2,1,0:T(4,128)(2,1)S(1)}, u32[]{:S(2)}, u32[]{:S(2)}) async-start(bf16[8,64,4,256]{3,2,1,0:T(4,128)(2,1)} %reshape.120), calls=%async_computation.5 | async-start | bytes 2097152 | tf_op jit(solution)/shard_map/all_to_all | solution.py:118
  246.7 12.6 %all-to-all-start.5 = ((bf16[8,2,64,256]{3,2,1,0:T(8,128)(2,1)}), bf16[8,2,64,256]{3,2,1,0:T(8,128)(2,1)}, u32[]{:S(2)}, u32[]{:S(2)}) async-start(bf16[8,2,64,256]{3,2,1,0:T(8,128)(2,1)} %copy.256), calls=%async_computation.8 | async-start | bytes 1048576 | tf_op jit(solution)/shard_map/all_to_all | solution.py:120
  256.7 170.7 %copy-start.1 = (bf16[1,1,8,64,4,256]{5,4,3,2,1,0:T(4,128)(2,1)S(1)}, bf16[1,1,8,64,4,256]{5,4,3,2,1,0:T(4,128)(2,1)}, u32[]{:S(2)}) copy-start(bf16[1,1,8,64,4,256]{5,4,3,2,1,0:T(4,128)(2,1)} %param.10) | copy-start | bytes 3145732
  (13 other events, 22.8 us)
Sparse Core Ops, SparseCore 0:
  11.2 93.2 all-gather.1
  183.3 13.8 reduce-scatter.3
  199.8 16.2 reduce-scatter.7
  219.8 206.0 reduce-scatter.5
where the time goes:
time: 440 us; the launch traced here: 434 us
  waiting for transfers between devices  245 us (56%)
  matrix products  61.5 us (14%)
  local copies, waits for them, and re-layouts  60.6 us (14%)
  starting transfers between devices  31.8 us (7%)
  other arithmetic  21.2 us (5%)
  between operations  14.5 us (3%)
    reduce_scatter x1, waiting for transfers between devices, body(): lax.psum_scatter(head_sum, 'prompt', scatter_dimension=1, tiled=True)  164 us
    unnamed x64, local copies, waits for them, and re-layouts  24.9 us
    all_gather x1, waiting for transfers between devices, body(): gathered = lax.all_gather(prompt_kv, 'prompt', axis=2, tiled=True)  21.9 us
    all_to_all x1, waiting for transfers between devices, body(): lax.all_to_all(out[:peers], 'resp', split_axis=0, concat_axis=0, tiled=True)  12.6 us
    all_to_all x1, waiting for transfers between devices, body(): lax.all_to_all(send_q, 'resp', split_axis=0, concat_axis=0, tiled=True)  12.4 us
    all_to_all x1, waiting for transfers between devices, body(): lax.all_to_all(send_grad, 'resp', split_axis=0, concat_axis=0, tiled=True)  12 us
    dot_general x1, matrix products, attend_blocks(): jnp.einsum('bkgrn,brkgd->nkd', w_sh, cotangent, preferred_element_type=f32)  10.9 us
    all_to_all x1, waiting for transfers between devices, body(): lax.all_to_all(send_kv, 'resp', split_axis=0, concat_axis=0, tiled=True)  10.8 us
  transfers between devices with their start and end apart: 10, of which 8 were waited for; matrix products, arithmetic and copies ran while one was open for 13% of the time, Pallas kernels for 0%

commit v1 on v0

--- a/solution.py
+++ b/solution.py
@@ -55,7 +55,9 @@
     resp_len = resp_q.shape[3]
     peers = lax.axis_size("resp")
     kv_width = kv_heads * head_size
-    gathered = lax.all_gather(prompt_kv, "prompt", axis=2, tiled=True)
+    gathered = jnp.concatenate(
+        lax.all_to_all(jnp.stack([prompt_kv] * lax.axis_size("prompt")), "prompt", 0, 0), axis=2
+    )
     prompt_keys = gathered[0, 0].reshape(full_len, kv_heads, head_size)
     prompt_values = gathered[1, 0].reshape(full_len, kv_heads, head_size)
     order = resp_prompt[0, 0]

time: 440 us -> 461 us (1.048)
  blocking collectives: 0 us -> 18.8 us
  local copies, waits for them, and re-layouts: 60.6 us -> 49.4 us
  starting transfers between devices: 31.8 us -> 38 us
  matrix products: 61.5 us -> 67.3 us
    all_to_all x1, waiting for transfers between devices: 12 us -> 34 us  [body(): lax.all_to_all(jnp.stack([prompt_kv] * lax.axis_size('prompt')), 'prompt'...]
    all_gather x1 -> x0, waiting for transfers between devices: 21.9 us -> none  [body(): gathered = lax.all_gather(prompt_kv, 'prompt', axis=2, tiled=True)]
    all_to_all x0 -> x1, blocking collectives: none -> 18.8 us  [body(): lax.all_to_all(send_grad, 'resp', split_axis=0, concat_axis=0, tiled=True)]
    unnamed x64 -> x61, local copies, waits for them, and re-layouts: 24.9 us -> 12.1 us
    another operation x0 -> x3, local copies, waits for them, and re-layouts: none -> 5.81 us  [the longest x1 2.14 us: body(): prompt_values = gathered[1, 0].reshape(full_len, kv_heads, head_size)]
    all_to_all x1, starting transfers between devices: 5.28 us -> 10.9 us  [body(): lax.all_to_all(jnp.stack([prompt_kv] * lax.axis_size('prompt')), 'prompt'...]
  transfers between devices with their start and end apart: 10 -> 9, of which waited for: 8 -> 8; matrix products, arithmetic and copies ran while one was open for 13% -> 11% of each run, Pallas kernels for 0% -> 0%
where the time goes in v1:
time: 461 us; the launch traced here: 456 us
  waiting for transfers between devices  247 us (54%)
  matrix products  67.3 us (15%)
  local copies, waits for them, and re-layouts  49.4 us (11%)
  starting transfers between devices  38 us (8%)
  other arithmetic  20.5 us (4%)
  blocking collectives  18.8 us (4%)
  between operations  14.5 us (3%)
    reduce_scatter x1, waiting for transfers between devices, body(): lax.psum_scatter(head_sum, 'prompt', scatter_dimension=1, tiled=True)  164 us
    all_to_all x1, waiting for transfers between devices, body(): lax.all_to_all(jnp.stack([prompt_kv] * lax.axis_size('prompt')), 'prompt'...  34 us
    all_to_all x1, blocking collectives, body(): lax.all_to_all(send_grad, 'resp', split_axis=0, concat_axis=0, tiled=True)  18.8 us
    dot_general x1, matrix products, attend_blocks(): jnp.einsum('brkgd,nkd->bkgrn', cotangent, values_in, preferred_element_ty...  14.1 us
    all_to_all x1, waiting for transfers between devices, body(): lax.all_to_all(send_kv, 'resp', split_axis=0, concat_axis=0, tiled=True)  12.6 us
    all_to_all x1, waiting for transfers between devices, body(): lax.all_to_all(out[:peers], 'resp', split_axis=0, concat_axis=0, tiled=True)  12.5 us
    unnamed x61, local copies, waits for them, and re-layouts  12.1 us
    all_to_all x1, waiting for transfers between devices, body(): lax.all_to_all(send_q, 'resp', split_axis=0, concat_axis=0, tiled=True)  11.5 us
  transfers between devices with their start and end apart: 9, of which 8 were waited for; matrix products, arithmetic and copies ran while one was open for 11% of the time, Pallas kernels for 0%

profile of v1, /device:TPU:8, one launch (start us, length us, event | category | flops | bytes accessed | tf_op | source)
XLA Modules:
  0.0 455.8 jit_solution(11504960595989508049)
XLA Ops:
  11.2 5.8 %all-to-all-start = ((bf16[8,64,4,256]{3,2,1,0:T(4,128)(2,1)}), bf16[8,64,4,256]{3,2,1,0:T(4,128)(2,1)S(1)}, u32[]{:S(2)}, u32[]{:S(2)}) async-start(bf16[8,64,4,256]{3,2,1,0:T(4,128)(2,1)} %copy.198), calls=%async_computation | async-start | bytes 2097152 | tf_op jit(solution)/shard_map/all_to_all | solution.py:75
  19.2 11.5 %all-to-all-done = bf16[8,64,4,256]{3,2,1,0:T(4,128)(2,1)S(1)} async-done(((bf16[8,64,4,256]{3,2,1,0:T(4,128)(2,1)}), bf16[8,64,4,256]{3,2,1,0:T(4,128)(2,1)S(1)}, u32[]{:S(2)}, u32[]{:S(2)}) %all-to-all-start) | async-done | bytes 1048608 | tf_op jit(solution)/shard_map/all_to_all | solution.py:75
  30.7 4.8 %all-to-all-start.2 = ((bf16[8,2,64,512]{3,2,1,0:T(8,128)(2,1)}), bf16[8,2,64,512]{3,2,1,0:T(8,128)(2,1)S(1)}, u32[]{:S(2)}, u32[]{:S(2)}) async-start(bf16[8,2,64,512]{3,2,1,0:T(8,128)(2,1)} %copy.204), calls=%async_computation.2 | async-start | bytes 2097152 | tf_op jit(solution)/shard_map/all_to_all | solution.py:76
  36.8 12.6 %all-to-all-done.2 = bf16[8,2,64,512]{3,2,1,0:T(8,128)(2,1)S(1)} async-done(((bf16[8,2,64,512]{3,2,1,0:T(8,128)(2,1)}), bf16[8,2,64,512]{3,2,1,0:T(8,128)(2,1)S(1)}, u32[]{:S(2)}, u32[]{:S(2)}) %all-to-all-start.2) | async-done | bytes 1048608 | tf_op jit(solution)/shard_map/all_to_all | solution.py:76
  49.3 18.8 %all_to_all.35 = bf16[8,64,4,256]{3,2,1,0:T(4,128)(2,1)} all-to-all(bf16[8,64,4,256]{3,2,1,0:T(4,128)(2,1)S(1)} %copy.221), channel_id=1, replica_groups=mesh['prompt'=16,'resp'=8,'head'=2] {'resp'}, dimensions={0} | all-to-all | bytes 2097152 | tf_op jit(solution)/shard_map/all_to_all | solution.py:77
  69.7 10.9 %all-to-all-start.1 = ((bf16[16,2,1,64,512]{4,3,2,1,0:T(8,128)(2,1)}), bf16[16,2,1,64,512]{4,3,2,1,0:T(8,128)(2,1)}, u32[]{:S(2)}, u32[]{:S(2)}) async-start(bf16[16,2,1,64,512]{4,3,2,1,0:T(8,128)(2,1)} %stack.14), calls=%async_computation.1 | async-start | bytes 4194304 | tf_op jit(solution)/shard_map/all_to_all | solution.py:59
  95.7 34.0 %all-to-all-done.1 = bf16[16,2,1,64,512]{4,3,2,1,0:T(8,128)(2,1)} async-done(((bf16[16,2,1,64,512]{4,3,2,1,0:T(8,128)(2,1)}), bf16[16,2,1,64,512]{4,3,2,1,0:T(8,128)(2,1)}, u32[]{:S(2)}, u32[]{:S(2)}) %all-to-all-start.1) | async-done | bytes 2097184 | tf_op jit(solution)/shard_map/all_to_all | solution.py:59
  129.7 3.1 fusion.64
  134.9 5.5 %bitcast_reduce_fusion = (f32[9,4,2,64]{3,2,0,1:T(2,128)S(1)}, f32[4,9,64,2,1024]{4,2,3,1,0:T(8,128)S(1)}) fusion(pred[9,64,1024]{2,1,0:T(8,128)(4,1)} %concatenate.17, bf16[1024,4,128,1,1]{2,1,0,4,3:T(4,128)(2,1)} %bitcast.153, bf16[9,64,4,2,128]{4,3,2,1,0:T(2,128)(2,1)} %reshape.128), kind=kOutput, calls=%fused_computation.5 | convolution fusion | flops 1222110720 | bytes 21710848 | tf_op jit(solution)/shard_map/brkgd,nkd->bkgrn/dot_general | solution.py:13
  140.5 5.4 %fusion.3 = f32[9,4,2,64]{3,2,0,1:T(2,128)S(1)} fusion(f32[4,9,64,2,1024]{4,2,3,1,0:T(8,128)S(1)} %get-tuple-element.43, f32[9,4,2,64]{3,2,0,1:T(2,128)S(1)} %copy.209, pred[9,64,1024]{2,1,0:T(8,128)(4,1)S(1)} %copy-done.13), kind=kLoop, calls=%fused_computation.7 | loop fusion | flops 18869760 | bytes 19501056 | tf_op jit(solution)/shard_map/reduce_sum | solution.py:20
  149.7 10.9 %fusion.28 = f32[4,128,1024,1,1]{2,1,4,3,0:T(8,128)} fusion(bf16[9,64,4,2,128]{4,3,2,1,0:T(2,128)(2,1)} %copy-done.3, f32[4,9,64,2,1024]{4,2,3,1,0:T(8,128)} %copy-done.2, f32[9,4,2,64]{3,2,0,1:T(2,128)S(1)} %copy.213, pred[9,64,1024]{2,1,0:T(8,128)(4,1)} %concatenate.17), kind=kOutput, calls=%fused_computation.54 | convolution fusion | flops 1226833920 | bytes 22759424 | tf_op jit(solution)/shard_map/bkgrn,brkgd->nkd/dot_general | solution.py:42
  162.8 10.4 %multiply_reduce_fusion = (f32[9,4,2,64]{3,2,0,1:T(2,128)S(1)}, bf16[9,64,4,2,128]{4,1,3,0,2:T(8,128)(2,1)}) fusion(f32[9,4,2,64,128]{4,2,3,1,0:T(2,128)S(1)} %copy-done.15, f32[9,4,128,2,64]{2,4,3,0,1:T(8,128)S(1)} %fusion.19, bf16[1024,4,128,1,1]{2,1,0,4,3:T(4,128)(2,1)S(1)} %bitcast.159, f32[4,9,64,2,1024]{4,2,3,1,0:T(8,128)} %copy-done.2, ...), kind=kOutput, calls=%fused_computation.21 | convolution fusion | flops 1229778432 | bytes 26447872 | tf_op jit(solution)/shard_map/bkgrn,nkd->brkgd/dot_general | solution.py:29
  173.2 14.1 %fusion.1 = bf16[9,4,2,64,1024]{4,3,2,0,1:T(8,128)(2,1)} fusion(f32[4,9,64,2,1024]{4,2,3,1,0:T(8,128)} %copy-done.2, f32[9,4,2,64]{3,2,0,1:T(2,128)S(1)} %get-tuple-element.44, f32[9,4,2,64]{3,2,0,1:T(2,128)S(1)} %copy.213, pred[9,64,1024]{2,1,0:T(8,128)(4,1)S(1)} %copy-done.14, bf16[9,64,4,2,128]{4,3,2,1,0:T(2,128)(2,1)S(1)} %copy-done.4, ...), kind=kOutput, calls=%fused_computation.2 | convolution fusion | flops 1236271104 | bytes 31166464 | tf_op jit(solution)/shard_map/brkgd,nkd->bkgrn/dot_general | solution.py:33
  187.3 6.7 %bitcast_multiply_fusion = f32[4,128,1024]{2,1,0:T(8,128)} fusion(bf16[9,4,2,64,1024]{4,3,2,0,1:T(8,128)(2,1)} %fusion.1, bf16[9,64,4,2,128]{4,3,2,1,0:T(2,128)(2,1)S(1)} %copy-done.6), kind=kOutput, calls=%fused_computation.25 | convolution fusion | flops 1208483840 | bytes 12713984 | tf_op jit(solution)/shard_map/bkgrn,brkgd->nkd/dot_general | solution.py:41
  194.0 2.9 copy.234
  196.9 3.0 copy.235
  199.9 4.6 %pad_maximum_fusion = f32[2,1024,512]{2,1,0:T(8,128)} fusion(f32[1,1024,512]{2,1,0:T(8,128)} %copy.235, f32[1,1024,512]{2,1,0:T(8,128)} %copy.234), kind=kLoop, calls=%fused_computation.11 | loop fusion | flops 1048576 | bytes 8388608 | tf_op jit(solution)/shard_map/stack | solution.py:110
  220.6 6.3 %fusion.7 = bf16[9,64,4,2,128]{4,1,3,0,2:T(8,128)(2,1)S(1)} fusion(f32[9,4,128,2,64]{2,4,3,0,1:T(8,128)S(1)} %fusion.17, bf16[9,4,2,64,1024]{4,3,2,0,1:T(8,128)(2,1)} %fusion.1, bf16[1024,4,128,1,1]{2,1,0,4,3:T(4,128)(2,1)S(1)} %bitcast.154), kind=kOutput, calls=%fused_computation.14 | convolution fusion | flops 1209729024 | bytes 14024704 | tf_op jit(solution)/shard_map/bkgrn,nkd->brkgd/dot_general | solution.py:38
  229.6 5.5 %all-to-all-start.5 = ((bf16[8,64,4,256]{3,2,1,0:T(4,128)(2,1)}), bf16[8,64,4,256]{3,2,1,0:T(4,128)(2,1)S(1)}, u32[]{:S(2)}, u32[]{:S(2)}) async-start(bf16[8,64,4,256]{3,2,1,0:T(4,128)(2,1)} %reshape.133), calls=%async_computation.7 | async-start | bytes 2097152 | tf_op jit(solution)/shard_map/all_to_all | solution.py:121
  237.8 11.1 %all-to-all-done.5 = bf16[8,64,4,256]{3,2,1,0:T(4,128)(2,1)S(1)} async-done(((bf16[8,64,4,256]{3,2,1,0:T(4,128)(2,1)}), bf16[8,64,4,256]{3,2,1,0:T(4,128)(2,1)S(1)}, u32[]{:S(2)}, u32[]{:S(2)}) %all-to-all-start.5) | async-done | bytes 1048608 | tf_op jit(solution)/shard_map/all_to_all | solution.py:121
  248.9 4.8 %all-to-all-start.4 = ((bf16[8,64,4,256]{3,2,1,0:T(4,128)(2,1)}), bf16[8,64,4,256]{3,2,1,0:T(4,128)(2,1)S(1)}, u32[]{:S(2)}, u32[]{:S(2)}) async-start(bf16[8,64,4,256]{3,2,1,0:T(4,128)(2,1)} %reshape.132), calls=%async_computation.6 | async-start | bytes 2097152 | tf_op jit(solution)/shard_map/all_to_all | solution.py:120
  255.9 12.5 %all-to-all-done.4 = bf16[8,64,4,256]{3,2,1,0:T(4,128)(2,1)S(1)} async-done(((bf16[8,64,4,256]{3,2,1,0:T(4,128)(2,1)}), bf16[8,64,4,256]{3,2,1,0:T(4,128)(2,1)S(1)}, u32[]{:S(2)}, u32[]{:S(2)}) %all-to-all-start.4) | async-done | bytes 1048608 | tf_op jit(solution)/shard_map/all_to_all | solution.py:120
  268.4 5.2 %all-to-all-start.6 = ((bf16[8,2,64,256]{3,2,1,0:T(8,128)(2,1)}), bf16[8,2,64,256]{3,2,1,0:T(8,128)(2,1)}, u32[]{:S(2)}, u32[]{:S(2)}) async-start(bf16[8,2,64,256]{3,2,1,0:T(8,128)(2,1)} %copy.246), calls=%async_computation.9 | async-start | bytes 1048576 | tf_op jit(solution)/shard_map/all_to_all | solution.py:122
  283.4 164.1 %reduce-scatter.6.cloned.1.call-done = f32[2,64,256]{2,1,0:T(8,128)} async-done(((f32[2,1024,256]{2,1,0:T(8,128)}), f32[2,64,256]{2,1,0:T(8,128)}) %reduce-scatter.6.cloned.1.call-update) | async-done | bytes 131088 | tf_op jit(solution)/shard_map/reduce_scatter | solution.py:112
  (127 shorter events, 66.7 us)
Async XLA Ops:
  9.8 7.2 %copy-start.19 = (bf16[2,1,1,8,64,512]{5,4,3,2,1,0:T(8,128)(2,1)S(1)}, bf16[2,1,1,8,64,512]{5,4,3,2,1,0:T(8,128)(2,1)}, u32[]{:S(2)}) copy-start(bf16[2,1,1,8,64,512]{5,4,3,2,1,0:T(8,128)(2,1)} %param.11) | copy-start | bytes 3145732
  9.9 7.2 %copy-start.26 = (s32[1,1,8]{2,1,0:T(1,128)S(1)}, s32[1,1,8]{2,1,0:T(1,128)}, u32[]{:S(2)}) copy-start(s32[1,1,8]{2,1,0:T(1,128)} %param.13) | copy-start | bytes 100
  11.2 19.5 %all-to-all-start = ((bf16[8,64,4,256]{3,2,1,0:T(4,128)(2,1)}), bf16[8,64,4,256]{3,2,1,0:T(4,128)(2,1)S(1)}, u32[]{:S(2)}, u32[]{:S(2)}) async-start(bf16[8,64,4,256]{3,2,1,0:T(4,128)(2,1)} %copy.198), calls=%async_computation | async-start | bytes 2097152 | tf_op jit(solution)/shard_map/all_to_all | solution.py:75
  17.9 17.6 %copy-start.20 = (bf16[1,1,8,64,4,256]{5,4,3,2,1,0:T(4,128)(2,1)S(1)}, bf16[1,1,8,64,4,256]{5,4,3,2,1,0:T(4,128)(2,1)}, u32[]{:S(2)}) copy-start(bf16[1,1,8,64,4,256]{5,4,3,2,1,0:T(4,128)(2,1)} %param.12) | copy-start | bytes 3145732
  30.7 18.6 %all-to-all-start.2 = ((bf16[8,2,64,512]{3,2,1,0:T(8,128)(2,1)}), bf16[8,2,64,512]{3,2,1,0:T(8,128)(2,1)S(1)}, u32[]{:S(2)}, u32[]{:S(2)}) async-start(bf16[8,2,64,512]{3,2,1,0:T(8,128)(2,1)} %copy.204), calls=%async_computation.2 | async-start | bytes 2097152 | tf_op jit(solution)/shard_map/all_to_all | solution.py:76
  36.3 31.9 %copy-start.22 = (bf16[2,1,64,512]{3,2,1,0:T(8,128)(2,1)S(1)}, bf16[2,1,64,512]{3,2,1,0:T(8,128)(2,1)}, u32[]{:S(2)}) copy-start(bf16[2,1,64,512]{3,2,1,0:T(8,128)(2,1)} %param.8) | copy-start | bytes 393220
  69.7 13.4 %copy-start.23 = (bf16[1,64,4,256]{3,2,1,0:T(4,128)(2,1)S(1)}, bf16[1,64,4,256]{3,2,1,0:T(4,128)(2,1)}, u32[]{:S(2)}) copy-start(bf16[1,64,4,256]{3,2,1,0:T(4,128)(2,1)} %param.7) | copy-start | bytes 393220
  69.7 60.0 %all-to-all-start.1 = ((bf16[16,2,1,64,512]{4,3,2,1,0:T(8,128)(2,1)}), bf16[16,2,1,64,512]{4,3,2,1,0:T(8,128)(2,1)}, u32[]{:S(2)}, u32[]{:S(2)}) async-start(bf16[16,2,1,64,512]{4,3,2,1,0:T(8,128)(2,1)} %stack.14), calls=%async_computation.1 | async-start | bytes 4194304 | tf_op jit(solution)/shard_map/all_to_all | solution.py:59
  80.7 138.3 %reduce-scatter.4.cloned.1.call-start = ((), (), s32[]{:S(2)}) async-start(), calls=%async_computation.10 | async-start | bytes 6291456 | tf_op jit(solution)/shard_map/reduce_scatter | solution.py:111
  91.3 3.2 copy-start.3
  91.8 2.7 copy-start.16
  91.8 2.7 copy-start.5
  91.8 2.7 copy-start.25
  134.9 5.6 %copy-start.13 = (pred[9,64,1024]{2,1,0:T(8,128)(4,1)S(1)}, pred[9,64,1024]{2,1,0:T(8,128)(4,1)}, u32[]{:S(2)}) copy-start(pred[9,64,1024]{2,1,0:T(8,128)(4,1)} %concatenate.17) | copy-start | bytes 1769476
  140.4 6.4 %copy-start.2 = (f32[4,9,64,2,1024]{4,2,3,1,0:T(8,128)}, f32[4,9,64,2,1024]{4,2,3,1,0:T(8,128)S(1)}, u32[]{:S(2)}) copy-start(f32[4,9,64,2,1024]{4,2,3,1,0:T(8,128)S(1)} %get-tuple-element.43) | copy-start | bytes 56623108
  162.8 10.4 %copy-start.4 = (bf16[9,64,4,2,128]{4,3,2,1,0:T(2,128)(2,1)S(1)}, bf16[9,64,4,2,128]{4,3,2,1,0:T(2,128)(2,1)}, u32[]{:S(2)}) copy-start(bf16[9,64,4,2,128]{4,3,2,1,0:T(2,128)(2,1)} %copy-done.3) | copy-start | bytes 3538948
  173.2 14.1 %copy-start.6 = (bf16[9,64,4,2,128]{4,3,2,1,0:T(2,128)(2,1)S(1)}, bf16[9,64,4,2,128]{4,3,2,1,0:T(2,128)(2,1)}, u32[]{:S(2)}) copy-start(bf16[9,64,4,2,128]{4,3,2,1,0:T(2,128)(2,1)} %reshape.128) | copy-start | bytes 3538948
  204.6 49.2 %reduce-scatter.8.cloned.1.call-start = ((), (), s32[]{:S(2)}) async-start(), calls=%async_computation.12 | async-start | bytes 3145728 | tf_op jit(solution)/shard_map/reduce_scatter | solution.py:116
  217.9 229.6 %reduce-scatter.6.cloned.1.call-start = ((), (), s32[]{:S(2)}) async-start(), calls=%async_computation.11 | async-start | bytes 2228224 | tf_op jit(solution)/shard_map/reduce_scatter | solution.py:112
  228.1 7.0 %copy-start.18 = (bf16[9,64,4,2,128]{4,1,3,0,2:T(8,128)(2,1)S(1)}, bf16[9,64,4,2,128]{4,1,3,0,2:T(8,128)(2,1)}, u32[]{:S(2)}) copy-start(bf16[9,64,4,2,128]{4,1,3,0,2:T(8,128)(2,1)} %get-tuple-element.45) | copy-start | bytes 3538948
  229.6 19.3 %all-to-all-start.5 = ((bf16[8,64,4,256]{3,2,1,0:T(4,128)(2,1)}), bf16[8,64,4,256]{3,2,1,0:T(4,128)(2,1)S(1)}, u32[]{:S(2)}, u32[]{:S(2)}) async-start(bf16[8,64,4,256]{3,2,1,0:T(4,128)(2,1)} %reshape.133), calls=%async_computation.7 | async-start | bytes 2097152 | tf_op jit(solution)/shard_map/all_to_all | solution.py:121
  248.9 19.5 %all-to-all-start.4 = ((bf16[8,64,4,256]{3,2,1,0:T(4,128)(2,1)}), bf16[8,64,4,256]{3,2,1,0:T(4,128)(2,1)S(1)}, u32[]{:S(2)}, u32[]{:S(2)}) async-start(bf16[8,64,4,256]{3,2,1,0:T(4,128)(2,1)} %reshape.132), calls=%async_computation.6 | async-start | bytes 2097152 | tf_op jit(solution)/shard_map/all_to_all | solution.py:120
  268.4 12.6 %all-to-all-start.6 = ((bf16[8,2,64,256]{3,2,1,0:T(8,128)(2,1)}), bf16[8,2,64,256]{3,2,1,0:T(8,128)(2,1)}, u32[]{:S(2)}, u32[]{:S(2)}) async-start(bf16[8,2,64,256]{3,2,1,0:T(8,128)(2,1)} %copy.246), calls=%async_computation.9 | async-start | bytes 1048576 | tf_op jit(solution)/shard_map/all_to_all | solution.py:122
  278.5 170.6 %copy-start.1 = (bf16[1,1,8,64,4,256]{5,4,3,2,1,0:T(4,128)(2,1)S(1)}, bf16[1,1,8,64,4,256]{5,4,3,2,1,0:T(4,128)(2,1)}, u32[]{:S(2)}) copy-start(bf16[1,1,8,64,4,256]{5,4,3,2,1,0:T(4,128)(2,1)} %param.10) | copy-start | bytes 3145732
  (12 other events, 17.7 us)
Sparse Core Ops, SparseCore 0:
  204.7 14.2 reduce-scatter.3
  221.6 16.2 reduce-scatter.7
  241.8 205.6 reduce-scatter.5
